TPU v7x, 256 devices: a whole 4x4x8 slice. The times are simulated.
256 devices in a mesh: wide: 32 (over x, y, z_lo), narrow: 8 (over z_hi, core).
Axes of the slice: x: 4, y: 4, z: 8 (z_hi: 4, z_lo: 2; z = z_hi * 2 + z_lo), core: 2. Of those that a mesh axis runs over, the one named last changes fastest.
Arguments:
- r_matrix: bfloat16 [10240, 102400], P('narrow', 'wide'), may hold values from -0.01953125 to 0.01953125
- cmm_panel: bfloat16 [102400, 1280], P('wide', 'narrow'), may hold values from -18 to 18
- ctm_panel: bfloat16 [10240, 1280], P('narrow', 'wide'), may hold values from -18 to 18
- cee_in: float32 [10240, 10240], P('wide', 'narrow'), may hold values from -2 to 2
Outputs:
- cee_out: float32 [10240, 10240], P('wide', 'narrow')
All inputs are finite; a program needn't handle non-finite values.
Results may differ from a plain program's by a relative error of at most 0.0022.
Values may be sent and summed in bfloat16 or wider, within the bound.
No kernel may reach another device: no remote copies, remote signals or barrier semaphores. Data moves between devices by JAX's collectives and lax.ppermute only.
A program may use at most 128 MiB of HBM per device.

v0:
```python
import jax
import jax.numpy as jnp
from jax import lax
from jax.sharding import PartitionSpec as P


def spread(value, axis, root):
    mine = lax.axis_index(axis) == root
    return lax.psum(jnp.where(mine, value, jnp.zeros_like(value)), axis)


def per_device(r_matrix, cmm_panel, ctm_panel, cee_in):
    slope_rows = r_matrix.shape[0]
    tile_rows = cee_in.shape[0]
    panel_width = ctm_panel.shape[1]
    r_panel = r_matrix[:, :panel_width]
    z_part = jnp.dot(
        r_matrix,
        lax.all_gather(cmm_panel, "narrow", axis=1, tiled=True),
        preferred_element_type=jnp.float32,
    )
    z_mine = lax.psum_scatter(z_part, "wide", scatter_dimension=1, tiled=True)
    a_mine = (z_mine - ctm_panel.astype(jnp.float32)).astype(jnp.bfloat16)
    a_whole, r_whole, c_whole = (
        lax.all_gather(a_mine, "wide", axis=1, tiled=True),
        lax.all_gather(r_panel, "wide", axis=1, tiled=True),
        lax.all_gather(ctm_panel, "wide", axis=1, tiled=True),
    )
    wide_index = lax.axis_index("wide")
    narrow_index = lax.axis_index("narrow")
    owner = wide_index * tile_rows // slope_rows
    offset = jnp.clip(wide_index * tile_rows - narrow_index * slope_rows, 0, slope_rows - tile_rows)
    a_rows = lax.dynamic_slice_in_dim(a_whole, offset, tile_rows, 0)
    r_rows = lax.dynamic_slice_in_dim(r_whole, offset, tile_rows, 0)
    left_rows = jnp.concatenate([a_rows, r_rows], axis=1)
    left_rows = spread(left_rows, "narrow", owner)
    right_cols = jnp.concatenate([r_whole, -c_whole], axis=1)
    update = lax.dot_general(
        left_rows, right_cols, (((1,), (1,)), ((), ())), preferred_element_type=jnp.float32
    )
    return cee_in + update


def solution(mesh):
    placed = (P("narrow", "wide"), P("wide", "narrow"), P("narrow", "wide"), P("wide", "narrow"))
    return jax.shard_map(
        per_device, mesh=mesh, in_specs=placed, out_specs=P("wide", "narrow"), check_vma=False
    )
```

profile of v0, /device:TPU:14, one launch (start us, length us, event | category | flops | bytes accessed | tf_op | source)
XLA Modules:
  0.0 891.5 jit_solution(11240906440603850587)
XLA Ops:
  6.5 0.0 all-gather.5.cloned.1.call-start
  6.5 0.7 all-gather.5.cloned.1.call-update
  7.3 0.0 reduce-scatter.2.cloned.1.call-start
  7.3 83.2 %all-gather.5.cloned.1.call-done = bf16[3200,1280]{0,1:T(8,128)(2,1)} async-done(((bf16[3200,160]{0,1:T(8,128)(2,1)}), bf16[3200,1280]{0,1:T(8,128)(2,1)}) %all-gather.5.cloned.1.call-update) | async-done | bytes 8192016 | tf_op jit(solution)/shard_map/all_gather | solution.py:19
  90.5 17.7 %fusion.8 = f32[1280,1280]{0,1:T(8,128)} fusion(bf16[1280,3200]{1,0:T(8,128)(2,1)} %param.4, bf16[3200,1280]{0,1:T(8,128)(2,1)} %all-gather.5.cloned.1.call-done), kind=kOutput, calls=%fused_computation.10 | convolution fusion | flops 10485760000 | bytes 22937600 | tf_op jit(solution)/shard_map/dot_general | solution.py:17
  108.2 0.0 slice-start
  108.2 0.0 copy-start
  108.2 0.0 reduce-scatter.2.cloned.1.call-update
  108.3 0.0 all-gather.9.cloned.1.call-start
  108.3 0.9 slice-done
  109.2 0.8 copy.6
  110.0 0.0 all-gather.9.cloned.1.call-update
  110.0 0.0 all-gather.7.cloned.1.call-start
  110.1 179.7 %reduce-scatter.2.cloned.1.call-done = f32[1280,40]{0,1:T(8,128)} async-done(((f32[1280,1280]{0,1:T(8,128)}), f32[1280,40]{0,1:T(8,128)}) %reduce-scatter.2.cloned.1.call-update) | async-done | bytes 204816 | tf_op jit(solution)/shard_map/reduce_scatter | solution.py:22
  289.7 0.0 copy-done
  289.7 1.6 subtract_convert_fusion
  291.3 0.0 all-gather.7.cloned.1.call-update
  291.4 0.0 all-gather.11.cloned.1.call-start
  291.4 0.5 all-gather.11.cloned.1.call-update
  291.9 0.0 all-reduce.2.cloned.1.call-start
  292.0 165.5 %all-gather.9.cloned.1.call-done = bf16[1280,1280]{0,1:T(8,128)(2,1)} async-done(((bf16[1280,40]{0,1:T(8,128)(2,1)}), bf16[1280,1280]{0,1:T(8,128)(2,1)}) %all-gather.9.cloned.1.call-update) | async-done | bytes 3276816 | tf_op jit(solution)/shard_map/all_gather | solution.py:26
  457.5 1.6 constant_dynamic-slice_fusion
  459.1 163.1 %all-gather.7.cloned.1.call-done = bf16[1280,1280]{0,1:T(8,128)(2,1)} async-done(((bf16[1280,40]{0,1:T(8,128)(2,1)}), bf16[1280,1280]{0,1:T(8,128)(2,1)}) %all-gather.7.cloned.1.call-update) | async-done | bytes 3276816 | tf_op jit(solution)/shard_map/all_gather | solution.py:25
  622.2 1.6 constant_dynamic-slice_fusion.1
  623.8 1.8 maximum_select_fusion
  625.6 0.0 all-reduce.2.cloned.1.call-update
  625.6 161.3 %all-gather.11.cloned.1.call-done = bf16[1280,1280]{0,1:T(8,128)(2,1)} async-done(((bf16[1280,40]{0,1:T(8,128)(2,1)}), bf16[1280,1280]{0,1:T(8,128)(2,1)}) %all-gather.11.cloned.1.call-update) | async-done | bytes 3276816 | tf_op jit(solution)/shard_map/all_gather | solution.py:27
  786.9 2.5 neg.3
  789.4 88.7 %all-reduce.2.cloned.1.call-done = bf16[320,2560]{0,1:T(8,128)(2,1)} async-done(((bf16[320,2560]{0,1:T(8,128)(2,1)}), bf16[320,2560]{0,1:T(8,128)(2,1)}) %all-reduce.2.cloned.1.call-update) | async-done | bytes 1638416 | tf_op jit(solution)/shard_map/psum | solution.py:9
  878.1 6.5 fusion.4
Async XLA Ops:
  6.5 83.9 %all-gather.5.cloned.1.call-start = ((), (), s32[]{:S(2)}) async-start(), calls=%async_computation.1 | async-start | bytes 9216000 | tf_op jit(solution)/shard_map/all_gather | solution.py:19
  7.3 282.5 %reduce-scatter.2.cloned.1.call-start = ((), (), s32[]{:S(2)}) async-start(), calls=%async_computation.2 | async-start | bytes 6758400 | tf_op jit(solution)/shard_map/reduce_scatter | solution.py:22
  108.2 1.0 slice-start
  108.2 181.5 %copy-start = (bf16[1280,40]{0,1:T(8,128)(2,1)S(1)}, bf16[1280,40]{0,1:T(8,128)(2,1)}, u32[]{:S(2)}) copy-start(bf16[1280,40]{0,1:T(8,128)(2,1)} %param.6) | copy-start | bytes 307204
  108.3 349.3 %all-gather.9.cloned.1.call-start = ((), (), s32[]{:S(2)}) async-start(), calls=%async_computation.4 | async-start | bytes 3379200 | tf_op jit(solution)/shard_map/all_gather | solution.py:26
  110.0 512.2 %all-gather.7.cloned.1.call-start = ((), (), s32[]{:S(2)}) async-start(), calls=%async_computation.3 | async-start | bytes 3379200 | tf_op jit(solution)/shard_map/all_gather | solution.py:25
  291.4 495.5 %all-gather.11.cloned.1.call-start = ((), (), s32[]{:S(2)}) async-start(), calls=%async_computation.6 | async-start | bytes 3379200 | tf_op jit(solution)/shard_map/all_gather | solution.py:27
  291.9 586.2 %all-reduce.2.cloned.1.call-start = ((), (), s32[]{:S(2)}) async-start(), calls=%async_computation.5 | async-start | bytes 3932160 | tf_op jit(solution)/shard_map/psum | solution.py:9
Sparse Core Ops, SparseCore 0:
  9.2 81.2 all-gather.4
  108.4 181.3 reduce-scatter.1
  291.5 165.9 all-gather.8
  459.2 163.0 all-gather.6
  623.8 163.0 all-gather.10
  789.4 88.6 all-reduce.1
where the time goes:
time: 892 us; the launch traced here: 891 us
  waiting for transfers between devices  843 us (95%)
  matrix products  24.2 us (3%)
  between operations  13.5 us (2%)
    reduce_scatter x1, waiting for transfers between devices, per_device(): z_mine = lax.psum_scatter(z_part, 'wide', scatter_dimension=1, tiled=True)  180 us
    all_gather x1, waiting for transfers between devices, per_device(): lax.all_gather(r_panel, 'wide', axis=1, tiled=True)  165 us
    all_gather x1, waiting for transfers between devices, per_device(): lax.all_gather(a_mine, 'wide', axis=1, tiled=True)  163 us
    all_gather x1, waiting for transfers between devices, per_device(): lax.all_gather(ctm_panel, 'wide', axis=1, tiled=True)  161 us
    psum x1, waiting for transfers between devices, spread(): return lax.psum(jnp.where(mine, value, jnp.zeros_like(value)), axis)  88.7 us
    all_gather x1, waiting for transfers between devices, per_device(): lax.all_gather(cmm_panel, 'narrow', axis=1, tiled=True)  83.2 us
  transfers between devices with their start and end apart: 6, of which 6 were waited for; matrix products, arithmetic and copies ran while one was open for 1% of the time, Pallas kernels for 0%

commit v1 on v0

--- a/solution.py
+++ b/solution.py
@@ -2,6 +2,16 @@
 import jax.numpy as jnp
 from jax import lax
 from jax.sharding import PartitionSpec as P
+
+write_the_face = lambda here_x, net_axis: jnp.concatenate(
+    lax.all_to_all(
+        jnp.stack(lax.axis_size(net_axis) * [here_x], 0),
+        axis_name=net_axis,
+        split_axis=0,
+        concat_axis=0,
+    ),
+    1,
+)
 
 
 def spread(value, axis, root):
@@ -22,7 +32,7 @@
     z_mine = lax.psum_scatter(z_part, "wide", scatter_dimension=1, tiled=True)
     a_mine = (z_mine - ctm_panel.astype(jnp.float32)).astype(jnp.bfloat16)
     a_whole, r_whole, c_whole = (
-        lax.all_gather(a_mine, "wide", axis=1, tiled=True),
+        write_the_face(a_mine, "wide"),
         lax.all_gather(r_panel, "wide", axis=1, tiled=True),
         lax.all_gather(ctm_panel, "wide", axis=1, tiled=True),
     )

time: 892 us -> 737 us (0.83)
  waiting for transfers between devices: 843 us -> 667 us
  starting transfers between devices: 0.2 us -> 18.7 us
    all_gather x1 -> x0, waiting for transfers between devices: 163 us -> none  [per_device(): lax.all_gather(a_mine, 'wide', axis=1, tiled=True)]
    all_to_all x0 -> x1, starting transfers between devices: none -> 18.5 us  [lax.all_to_all(jnp.stack(lax.axis_size(net_axis) * [here_x], 0), axis_nam...]
    all_gather x1, waiting for transfers between devices: 165 us -> 152 us  [per_device(): lax.all_gather(r_panel, 'wide', axis=1, tiled=True)]
  transfers between devices with their start and end apart: 6 -> 6, of which waited for: 6 -> 5; matrix products, arithmetic and copies ran while one was open for 1% -> 2% of each run, Pallas kernels for 0% -> 0%
where the time goes in v1:
time: 737 us; the launch traced here: 736 us
  waiting for transfers between devices  667 us (91%)
  matrix products  24.2 us (3%)
  starting transfers between devices  18.7 us (3%)
  between operations  13.2 us (2%)
    reduce_scatter x1, waiting for transfers between devices, per_device(): z_mine = lax.psum_scatter(z_part, 'wide', scatter_dimension=1, tiled=True)  180 us
    all_gather x1, waiting for transfers between devices, per_device(): lax.all_gather(ctm_panel, 'wide', axis=1, tiled=True)  161 us
    all_gather x1, waiting for transfers between devices, per_device(): lax.all_gather(r_panel, 'wide', axis=1, tiled=True)  152 us
    psum x1, waiting for transfers between devices, spread(): return lax.psum(jnp.where(mine, value, jnp.zeros_like(value)), axis)  89.1 us
    all_gather x1, waiting for transfers between devices, per_device(): lax.all_gather(cmm_panel, 'narrow', axis=1, tiled=True)  83.2 us
    all_to_all x1, starting transfers between devices, lax.all_to_all(jnp.stack(lax.axis_size(net_axis) * [here_x], 0), axis_nam...  18.5 us
    dot_general x1, matrix products, per_device(): jnp.dot(r_matrix, lax.all_gather(cmm_panel, 'narrow', axis=1, tiled=True)...  17.7 us
  transfers between devices with their start and end apart: 6, of which 5 were waited for; matrix products, arithmetic and copies ran while one was open for 2% of the time, Pallas kernels for 0%

profile of v1, /device:TPU:14, one launch (start us, length us, event | category | flops | bytes accessed | tf_op | source)
XLA Modules:
  0.0 736.4 jit_solution(11738345147949729921)
XLA Ops:
  6.5 0.0 all-gather.4.cloned.1.call-start
  6.5 0.7 all-gather.4.cloned.1.call-update
  7.3 0.0 reduce-scatter.2.cloned.1.call-start
  7.3 83.2 %all-gather.4.cloned.1.call-done = bf16[3200,1280]{0,1:T(8,128)(2,1)} async-done(((bf16[3200,160]{0,1:T(8,128)(2,1)}), bf16[3200,1280]{0,1:T(8,128)(2,1)}) %all-gather.4.cloned.1.call-update) | async-done | bytes 8192016 | tf_op jit(solution)/shard_map/all_gather | solution.py:29
  90.5 17.7 %fusion.8 = f32[1280,1280]{0,1:T(8,128)} fusion(bf16[1280,3200]{1,0:T(8,128)(2,1)} %param.4, bf16[3200,1280]{0,1:T(8,128)(2,1)} %all-gather.4.cloned.1.call-done), kind=kOutput, calls=%fused_computation.10 | convolution fusion | flops 10485760000 | bytes 22937600 | tf_op jit(solution)/shard_map/dot_general | solution.py:27
  108.2 0.0 slice-start
  108.2 0.0 copy-start
  108.2 0.0 reduce-scatter.2.cloned.1.call-update
  108.3 0.0 all-gather.6.cloned.1.call-start
  108.3 0.9 slice-done
  109.2 0.8 copy.6
  110.0 0.0 all-gather.6.cloned.1.call-update
  110.0 180.3 %reduce-scatter.2.cloned.1.call-done = f32[1280,40]{0,1:T(8,128)} async-done(((f32[1280,1280]{0,1:T(8,128)}), f32[1280,40]{0,1:T(8,128)}) %reduce-scatter.2.cloned.1.call-update) | async-done | bytes 204816 | tf_op jit(solution)/shard_map/reduce_scatter | solution.py:32
  290.3 0.0 copy-done
  290.3 0.9 subtract_convert_fusion
  291.3 2.0 stack.2
  293.2 18.5 %all-to-all-start = ((bf16[32,1280,40]{1,2,0:T(8,128)(2,1)}), bf16[32,1280,40]{1,2,0:T(8,128)(2,1)S(1)}, u32[]{:S(2)}, u32[]{:S(2)}) async-start(bf16[32,1280,40]{1,2,0:T(8,128)(2,1)} %stack.2), calls=%async_computation.1 | async-start | bytes 6553600 | tf_op jit(solution)/shard_map/all_to_all | solution.py:7
  311.7 0.0 all-gather.8.cloned.1.call-start
  311.8 0.5 all-gather.8.cloned.1.call-update
  312.3 0.0 all-reduce.2.cloned.1.call-start
  312.4 152.3 %all-gather.6.cloned.1.call-done = bf16[1280,1280]{0,1:T(8,128)(2,1)} async-done(((bf16[1280,40]{0,1:T(8,128)(2,1)}), bf16[1280,1280]{0,1:T(8,128)(2,1)}) %all-gather.6.cloned.1.call-update) | async-done | bytes 3276816 | tf_op jit(solution)/shard_map/all_gather | solution.py:36
  464.7 2.5 constant_dynamic-slice_fusion
  467.2 0.0 all-to-all-done
  467.2 0.4 constant_dynamic-slice_fusion.1
  467.6 3.0 maximum_select_fusion
  470.6 0.0 all-reduce.2.cloned.1.call-update
  470.6 161.2 %all-gather.8.cloned.1.call-done = bf16[1280,1280]{0,1:T(8,128)(2,1)} async-done(((bf16[1280,40]{0,1:T(8,128)(2,1)}), bf16[1280,1280]{0,1:T(8,128)(2,1)}) %all-gather.8.cloned.1.call-update) | async-done | bytes 3276816 | tf_op jit(solution)/shard_map/all_gather | solution.py:37
  631.7 2.5 neg.3
  634.3 89.1 %all-reduce.2.cloned.1.call-done = bf16[320,2560]{0,1:T(8,128)(2,1)} async-done(((bf16[320,2560]{0,1:T(8,128)(2,1)}), bf16[320,2560]{0,1:T(8,128)(2,1)}) %all-reduce.2.cloned.1.call-update) | async-done | bytes 1638416 | tf_op jit(solution)/shard_map/psum | solution.py:19
  723.4 6.5 fusion.4
Async XLA Ops:
  6.5 83.9 %all-gather.4.cloned.1.call-start = ((), (), s32[]{:S(2)}) async-start(), calls=%async_computation.2 | async-start | bytes 9216000 | tf_op jit(solution)/shard_map/all_gather | solution.py:29
  7.3 283.1 %reduce-scatter.2.cloned.1.call-start = ((), (), s32[]{:S(2)}) async-start(), calls=%async_computation.3 | async-start | bytes 6758400 | tf_op jit(solution)/shard_map/reduce_scatter | solution.py:32
  108.2 1.0 slice-start
  108.2 182.1 %copy-start = (bf16[1280,40]{0,1:T(8,128)(2,1)S(1)}, bf16[1280,40]{0,1:T(8,128)(2,1)}, u32[]{:S(2)}) copy-start(bf16[1280,40]{0,1:T(8,128)(2,1)} %param.6) | copy-start | bytes 307204
  108.3 356.4 %all-gather.6.cloned.1.call-start = ((), (), s32[]{:S(2)}) async-start(), calls=%async_computation.4 | async-start | bytes 3379200 | tf_op jit(solution)/shard_map/all_gather | solution.py:36
  293.2 174.0 %all-to-all-start = ((bf16[32,1280,40]{1,2,0:T(8,128)(2,1)}), bf16[32,1280,40]{1,2,0:T(8,128)(2,1)S(1)}, u32[]{:S(2)}, u32[]{:S(2)}) async-start(bf16[32,1280,40]{1,2,0:T(8,128)(2,1)} %stack.2), calls=%async_computation.1 | async-start | bytes 6553600 | tf_op jit(solution)/shard_map/all_to_all | solution.py:7
  311.7 320.0 %all-gather.8.cloned.1.call-start = ((), (), s32[]{:S(2)}) async-start(), calls=%async_computation.6 | async-start | bytes 3379200 | tf_op jit(solution)/shard_map/all_gather | solution.py:37
  312.3 411.1 %all-reduce.2.cloned.1.call-start = ((), (), s32[]{:S(2)}) async-start(), calls=%async_computation.5 | async-start | bytes 3932160 | tf_op jit(solution)/shard_map/psum | solution.py:19
Sparse Core Ops, SparseCore 0:
  9.2 81.2 all-gather.3
  108.4 181.8 reduce-scatter.1
  292.1 172.5 all-gather.5
  466.3 165.3 all-gather.7
  634.3 89.0 all-reduce.1
